TPU v7x, 32 devices: a whole 2x2x4 slice. The times are simulated.
32 devices in a mesh: groups: 2 (over y), gx: 4 (over z), gy: 2 (over x), gz: 2 (over core).
Axes of the slice: x: 2, y: 2, z: 4, core: 2. Of those that a mesh axis runs over, the one named last changes fastest.
Arguments:
- parent: bfloat16 [160, 32, 1024], P('groups', 'gx', ('gy', 'gz')), parts along dimension 0, may hold values from -6 to 6
- nest: bfloat16 [160, 24, 1536], P('groups', 'gx', ('gy', 'gz')), parts along dimension 0, may hold values from -6 to 6
- nu_parent: float32 [80], replicated, may hold values from 0.03 to 0.24
- nu_nest: float32 [80], replicated, may hold values from 0.03 to 0.24
- relax: float32 [80], replicated, may hold values from 0.1 to 0.5
- feedback: float32 [80], replicated, may hold values from 0.3 to 1
- vert_mix: float32 [80, 80], replicated, may hold values from -1 to 1
- fp_owner: int32 [4, 4, 256, 1], P('gx', ('gy', 'gz')), may hold values from 0 to 3; in each aligned block of 256 rows (0 to 255, 256 to 511, ..., all dimensions but the last counted through in order) at most 256 rows name the same one
- fp_cell: int32 [4, 4, 256], P('gx', ('gy', 'gz')), may hold values from 0 to 2047
- nest_of: int32 [24], replicated, may hold values from 0 to 2, as said below
Outputs:
- parent_out: bfloat16 [160, 32, 1024], P('groups', 'gx', ('gy', 'gz')), parts along dimension 0
- nest_out: bfloat16 [160, 24, 1536], P('groups', 'gx', ('gy', 'gz')), parts along dimension 0
There are 2 independent parts, one for each index of `groups`. A program takes and returns all parts, laid end to end along the dimension named above; an argument that names none is the same for every part. Nothing has to cross between parts.
Inputs may be any that keep to these rules, and one draw needn't show every extreme that they name: `fp_owner`: within the 256 blocks of one nest tile no parent tile is named more than 256 times; in some nest tiles one is named exactly 256 times. `nest_of`: never falls along the rows; every nest holds one or more rows; nest 1 holds rows 11 and 12.
All inputs are finite; a program needn't handle non-finite values.
Results may differ from a plain program's by a relative error of at most 0.0033.
Values may be sent and summed in bfloat16 or wider, within the bound.
No kernel may reach another device: no remote copies, remote signals or barrier semaphores. Data moves between devices by JAX's collectives and lax.ppermute only.
A program may use at most 64 MiB of HBM per device.

v0:
```python
import jax
import jax.numpy as jnp
from jax import lax
from jax.sharding import PartitionSpec as P

Y_AXES = ("gy", "gz")
HI = lax.Precision.HIGHEST


def shift_pairs(count):
    forward = [(i, i + 1) for i in range(count - 1)]
    backward = [(i + 1, i) for i in range(count - 1)]
    return (forward, backward)


def exchange(blocks):
    fwd_x, bwd_x = shift_pairs(lax.axis_size("gx"))
    fwd_y, bwd_y = shift_pairs(lax.axis_size(Y_AXES))
    last_rows = jnp.concatenate([b[:, -1, :] for b in blocks], axis=1)
    first_rows = jnp.concatenate([b[:, 0, :] for b in blocks], axis=1)
    last_cols = jnp.concatenate([b[:, :, -1] for b in blocks], axis=1)
    first_cols = jnp.concatenate([b[:, :, 0] for b in blocks], axis=1)
    above = lax.ppermute(last_rows, "gx", fwd_x)
    below = lax.ppermute(first_rows, "gx", bwd_x)
    left = lax.ppermute(last_cols, Y_AXES, fwd_y)
    right = lax.ppermute(first_cols, Y_AXES, bwd_y)
    out = []
    xo = 0
    yo = 0
    for b in blocks:
        w, h = (b.shape[2], b.shape[1])
        out.append(
            (
                above[:, xo : xo + w],
                below[:, xo : xo + w],
                left[:, yo : yo + h],
                right[:, yo : yo + h],
            )
        )
        xo += w
        yo += h
    return out


def per_row(values, rows, cols):
    if values.ndim == 1:
        return jnp.broadcast_to(values[:, None], (rows, cols)).reshape(rows * cols)
    return jnp.broadcast_to(values[:, :, None], values.shape + (cols,)).reshape(
        values.shape[0], rows * cols
    )


def flat_stencil(flat, rows, cols, halo, up_w=None, down_w=None):
    above, below, left, right = (h.astype(flat.dtype) for h in halo)
    levels = flat.shape[0]
    up = jnp.concatenate([above, flat[:, :-cols]], axis=1)
    down = jnp.concatenate([flat[:, cols:], below], axis=1)
    col = lax.broadcasted_iota(jnp.int32, (1, rows * cols), 1) % cols
    zero = jnp.zeros((levels, 1), flat.dtype)
    west = jnp.where(
        col == 0, per_row(left, rows, cols), jnp.concatenate([zero, flat[:, :-1]], axis=1)
    )
    east = jnp.where(
        col == cols - 1, per_row(right, rows, cols), jnp.concatenate([flat[:, 1:], zero], axis=1)
    )
    if down_w is not None:
        down = down * down_w[None, :]
        up = up * up_w[None, :]
    return down + up + east + west - 4.0 * flat


def mix_levels(matrix, flat):
    return jnp.dot(matrix, flat, precision=HI, preferred_element_type=jnp.float32)


def nest_segments(nest_of, first, count):
    index_rows = first + jnp.arange(count, dtype=jnp.int32)
    inside = (index_rows >= 0) & (index_rows < nest_of.shape[0])
    return jnp.where(inside, nest_of[jnp.clip(index_rows, 0, nest_of.shape[0] - 1)], -1)


def row_weights(segments):
    left_w = (segments[:-2] == segments[1:-1]).astype(jnp.float32)
    right_w = (segments[2:] == segments[1:-1]).astype(jnp.float32)
    return (left_w, right_w)


def block_expansion(block_rows, block_cols, rows, cols, zero):
    r = lax.broadcasted_iota(jnp.int32, (block_rows * block_cols, rows * cols), 0) + zero
    p = lax.broadcasted_iota(jnp.int32, (block_rows * block_cols, rows * cols), 1)
    hit = (p // cols // 3 == r // block_cols) & (p % cols // 3 == r % block_cols)
    return hit.astype(jnp.float32)


def body(parent, nest, nu_parent, nu_nest, relax, feedback, vert_mix, fp_owner, fp_cell, nest_of):
    levels, p_rows, p_cols = parent.shape
    _, n_rows, n_cols = nest.shape
    tiles_x = lax.axis_size("gx")
    here_x = lax.axis_index("gx")
    zero = jnp.minimum(here_x, 0)
    parent_halo, nest_halo = exchange([parent, nest])
    centre = parent.astype(jnp.float32).reshape(levels, p_rows * p_cols)
    stencil = flat_stencil(centre, p_rows, p_cols, parent_halo)
    flat_parent = mix_levels(vert_mix, centre + nu_parent[:, None] * stencil)
    owners = fp_owner.reshape(-1)
    cells = fp_cell.reshape(-1)
    requests = owners.shape[0]
    slots = 4 * requests // tiles_x
    owner_ids = jnp.arange(tiles_x, dtype=jnp.int32)
    if slots >= requests:
        chosen = owners[None, :] == owner_ids[:, None]
        wanted = jnp.where(chosen, cells[None, :], 0)
        wanted = jnp.pad(wanted, ((0, 0), (0, slots - requests))).reshape(-1)
    else:
        onehot = (owners[:, None] == owner_ids[None, :]).astype(jnp.int32)
        before = jnp.cumsum(onehot, axis=0) - onehot
        order_in = jnp.sum(before * onehot, axis=1)
        places = owners * slots + order_in
        wanted = jnp.zeros((tiles_x * slots,), jnp.int32).at[places].set(cells)
    served_ids = lax.all_to_all(wanted, "gx", split_axis=0, concat_axis=0, tiled=True)
    answers = lax.all_to_all(
        jnp.take(flat_parent, served_ids, axis=1), "gx", split_axis=1, concat_axis=1, tiled=True
    )
    if slots >= requests:
        answers = answers.reshape(levels, tiles_x, slots)[:, :, :requests]
        forcing_flat = answers[:, 0, :]
        for o in range(1, tiles_x):
            forcing_flat = jnp.where(chosen[o][None, :], answers[:, o, :], forcing_flat)
    else:
        forcing_flat = jnp.take(answers, places, axis=1)
    block_rows = n_rows // 3
    block_cols = n_cols // 3
    expand = block_expansion(block_rows, block_cols, n_rows, n_cols, zero)
    forcing_full = jnp.dot(forcing_flat, expand, precision=HI, preferred_element_type=jnp.float32)
    row_start = here_x * n_rows
    left_w, right_w = row_weights(nest_segments(nest_of, row_start - 1, n_rows + 2))
    up_w = per_row(left_w, n_rows, n_cols)
    down_w = per_row(right_w, n_rows, n_cols)
    nest_state = nest.astype(jnp.float32).reshape(levels, n_rows * n_cols)
    halo = nest_halo
    for turn_no in range(3):
        if turn_no > 0:
            shaped = nest_state.astype(jnp.bfloat16).reshape(levels, n_rows, n_cols)
            (halo,) = exchange([shaped])
        stencil_sum = flat_stencil(nest_state, n_rows, n_cols, halo, up_w, down_w)
        moved = nest_state + nu_nest[:, None] * stencil_sum
        moved = moved + relax[:, None] * (forcing_full - moved)
        nest_state = mix_levels(vert_mix, moved)
    block_sum = lax.dot_general(
        nest_state,
        expand,
        (((1,), (1,)), ((), ())),
        precision=HI,
        preferred_element_type=jnp.float32,
    )
    nudge_gap = block_sum / 9.0 - forcing_flat
    if slots >= requests:
        outgoing = jnp.where(chosen[None, :, :], nudge_gap[:, None, :], 0.0)
        outgoing = jnp.pad(outgoing, ((0, 0), (0, 0), (0, slots - requests)))
        outgoing = outgoing.reshape(levels, tiles_x * slots)
    else:
        outgoing = jnp.zeros((levels, tiles_x * slots), jnp.float32).at[:, places].set(nudge_gap)
    incoming = lax.all_to_all(outgoing, "gx", split_axis=1, concat_axis=1, tiled=True)
    summed = jnp.zeros_like(flat_parent).at[:, served_ids].add(incoming)
    parent_out = (flat_parent + feedback[:, None] * summed).astype(jnp.bfloat16)
    return (
        parent_out.reshape(levels, p_rows, p_cols),
        nest_state.astype(jnp.bfloat16).reshape(levels, n_rows, n_cols),
    )


def solution(mesh):
    placed = (
        P("groups", "gx", Y_AXES),
        P("groups", "gx", Y_AXES),
        P(),
        P(),
        P(),
        P(),
        P(),
        P("gx", Y_AXES, None, None),
        P("gx", Y_AXES, None),
        P(),
    )
    return jax.shard_map(
        body,
        mesh=mesh,
        in_specs=placed,
        out_specs=(P("groups", "gx", Y_AXES), P("groups", "gx", Y_AXES)),
        check_vma=False,
    )
```

profile of v0, /device:TPU:1, one launch (start us, length us, event | category | flops | bytes accessed | tf_op | source)
XLA Modules:
  0.0 121.2 jit_solution(3893287503478127455)
XLA Ops:
  0.7 0.9 slice_bitcast_fusion.4
  1.6 1.2 %fusion.144 = (bf16[80,1,256]{2,1,0:T(2,128)(2,1)S(1)}, bf16[80,1,256]{2,1,0:T(2,128)(2,1)S(1)}) fusion(bf16[80,8,256]{2,1,0:T(8,128)(2,1)} %param.10), kind=kLoop, calls=%fused_computation.220 | loop fusion | bytes 163840 | tf_op jit(solution)/shard_map/slice | solution.py:19
  2.8 0.7 pad_maximum_fusion
  3.5 1.4 %collective-permute-start = (bf16[80,640]{1,0:T(8,128)(2,1)}, bf16[80,640]{1,0:T(8,128)(2,1)}, u32[]{:S(2)}, u32[]{:S(2)}) collective-permute-start(bf16[80,640]{1,0:T(8,128)(2,1)} %pad_maximum_fusion), channel_id=1, source_target_pairs={{4,0},{8,4},{12,8},{5,1},{9,5},{13,9},{6,2},{10,6},{14,10},{7,3},{... | collective-permute-start | bytes 307208 | tf_op jit(solution)/shard_map/ppermute | solution.py:24
  4.9 0.7 pad_maximum_fusion.1
  5.6 5.3 %collective-permute-start.1 = (bf16[80,640]{1,0:T(8,128)(2,1)}, bf16[80,640]{1,0:T(8,128)(2,1)}, u32[]{:S(2)}, u32[]{:S(2)}) collective-permute-start(bf16[80,640]{1,0:T(8,128)(2,1)} %pad_maximum_fusion.1), channel_id=1, source_target_pairs={{0,4},{4,8},{8,12},{1,5},{5,9},{9,13},{2,6},{6,10},{10,14},{3,7},{... | collective-permute-start | bytes 307208 | tf_op jit(solution)/shard_map/ppermute | solution.py:23
  11.4 4.4 %collective-permute-start.3 = (bf16[80,14]{0,1:T(8,128)(2,1)S(1)}, bf16[80,14]{0,1:T(8,128)(2,1)S(1)}, u32[]{:S(2)}, u32[]{:S(2)}) collective-permute-start(bf16[80,14]{0,1:T(8,128)(2,1)S(1)} %pad_maximum_fusion.3), channel_id=1, source_target_pairs={{0,1},{1,2},{2,3},{4,5},{5,6},{6,7},{8,9},{9,10},{10,11},{12,13},{... | collective-permute-start | bytes 6728 | tf_op jit(solution)/shard_map/ppermute | solution.py:25
  16.1 1.9 %collective-permute-start.2 = (bf16[80,14]{0,1:T(8,128)(2,1)S(1)}, bf16[80,14]{0,1:T(8,128)(2,1)S(1)}, u32[]{:S(2)}, u32[]{:S(2)}) collective-permute-start(bf16[80,14]{0,1:T(8,128)(2,1)S(1)} %pad_maximum_fusion.2), channel_id=1, source_target_pairs={{1,0},{2,1},{3,2},{5,4},{6,5},{7,6},{9,8},{10,9},{11,10},{13,12},{... | collective-permute-start | bytes 6728 | tf_op jit(solution)/shard_map/ppermute | solution.py:26
  18.1 0.6 compare_select_fusion.1
  18.7 3.6 %all-to-all-start = ((s32[4,256,1]{1,2,0:T(1,128)}), s32[4,256,1]{1,2,0:T(1,128)S(1)}, u32[]{:S(2)}, u32[]{:S(2)}) async-start(s32[4,256,1]{1,2,0:T(1,128)} %compare_select_fusion.1), calls=%async_computation | async-start | bytes 8192 | tf_op jit(solution)/shard_map/all_to_all | solution.py:120
  22.3 1.1 fusion.137
  23.9 1.1 fusion.135
  25.0 1.4 %fusion.134 = (f32[80,2303]{1,0:T(8,128)}, f32[80,2303]{1,0:T(8,128)}) fusion(f32[80,2304]{1,0:T(8,128)S(1)} %bitcast.111), kind=kLoop, calls=%fused_computation.210 | loop fusion | bytes 2947840 | tf_op jit(solution)/shard_map/slice | solution.py:64
  26.4 0.6 gather_fusion
  27.2 2.2 %fusion.6 = pred[256,2304]{1,0:T(32,128)(4,1)} fusion(s32[256]{0:T(256)S(1)} %get-tuple-element.58, s32[256]{0:T(256)S(1)} %get-tuple-element.59, s32[2304]{0:T(1024)S(1)} %get-tuple-element.62, s32[2304]{0:T(1024)S(1)} %get-tuple-element.63, s32[256]{0:T(256)S(1)} %get-tuple-element.57, s32[256]{0:T(256)S(1)} %get-tuple-element.60, ...), kind=kLoop, calls=%fused_computation.20 | loop fusion | flops 13565952 | bytes 635904 | tf_op jit(solution)/shard_map/and | solution.py:91
  29.8 1.0 copy.130
  31.1 1.0 copy.129
  32.2 0.8 slice_convert_fusion.3
  33.0 0.8 slice_convert_fusion.2
  33.8 2.8 %convolution_bitcast_fusion.2 = f32[80,2048]{1,0:T(8,128)S(1)} fusion(f32[80,80]{1,0:T(8,128)S(1)} %copy-done, f32[80,2048]{1,0:T(8,128)S(1)} %bitcast.115, f32[80,256]{1,0:T(8,128)S(1)} %slice_convert_fusion.3, f32[80,1792]{1,0:T(8,128)} %get-tuple-element.28, f32[80,1792]{1,0:T(8,128)} %get-tuple-element.27, f32[80,256]{1,0:T(8,128)S(1)} %slice_convert_fusion.2, ...), kind=kOutput, calls=%fused_computation.13 | convolution fusion | flops 159088640 | bytes 5272256 | tf_op jit(solution)/shard_map/dot_general | solution.py:73
  36.6 0.3 copy.93
  36.9 2.8 %gather_fusion.1 = f32[1024,80]{1,0:T(8,128)S(1)} fusion(f32[80,2048]{0,1:T(8,128)S(1)} %copy.93, s32[1024]{0:T(1024)S(1)} %broadcast_clamp_fusion), kind=kCustom, calls=%fused_computation.1 | custom fusion | bytes 659456 | tf_op jit(solution)/shard_map/jit(_take)/gather | solution.py:122
  39.9 0.8 broadcast_select_fusion.1
  40.7 4.5 %all-to-all-start.1 = ((f32[80,4,256]{2,0,1:T(8,128)}), f32[80,4,256]{2,0,1:T(8,128)S(1)}, u32[]{:S(2)}, u32[]{:S(2)}) async-start(f32[80,4,256]{2,0,1:T(8,128)} %broadcast_select_fusion.1), calls=%async_computation.1 | async-start | bytes 655360 | tf_op jit(solution)/shard_map/all_to_all | solution.py:121
  45.5 1.0 copy.132
  46.8 1.0 copy.131
  47.8 1.5 %slice_convert_fusion = f32[80,384]{1,0:T(8,128)} fusion(bf16[80,640]{1,0:T(8,128)(2,1)} %collective-permute-done.1), kind=kLoop, calls=%fused_computation.131 | loop fusion | flops 30720 | bytes 184320 | tf_op jit(solution)/shard_map/convert_element_type | solution.py:54
  49.3 1.6 %slice_convert_fusion.1 = f32[80,384]{1,0:T(8,128)} fusion(bf16[80,640]{1,0:T(8,128)(2,1)} %collective-permute-done), kind=kLoop, calls=%fused_computation.132 | loop fusion | flops 30720 | bytes 184320 | tf_op jit(solution)/shard_map/convert_element_type | solution.py:54
  50.8 3.9 %all-to-all-done.1 = f32[80,4,256]{2,0,1:T(8,128)S(1)} async-done(((f32[80,4,256]{2,0,1:T(8,128)}), f32[80,4,256]{2,0,1:T(8,128)S(1)}, u32[]{:S(2)}, u32[]{:S(2)}) %all-to-all-start.1) | async-done | bytes 327712 | tf_op jit(solution)/shard_map/all_to_all | solution.py:121
  54.8 0.8 fusion.148
  55.7 3.3 %fusion.145 = (bf16[80,2304]{1,0:T(8,128)(2,1)S(1)}, f32[80,2304]{1,0:T(8,128)S(1)}) fusion(f32[80,80]{1,0:T(8,128)S(1)} %copy-done, f32[80,2304]{1,0:T(8,128)S(1)} %fusion.148, f32[80,2304]{1,0:T(8,128)S(1)} %bitcast.112, f32[80,1920]{1,0:T(8,128)} %get-tuple-element.23, f32[80,384]{1,0:T(8,128)S(1)} %copy-done.16, f32[80,384]{1,0:T(8,128)S(1)} %copy-done.17, ...), kind=kOutput, calls=%fused_computation.221 | convolution fusion | flops 180080640 | bytes 7052800 | tf_op jit(solution)/shard_map/dot_general | solution.py:73
  59.0 0.4 reshape.289
  59.7 1.3 %collective-permute-start.5 = (bf16[80,384]{1,0:T(8,128)(2,1)S(1)}, bf16[80,384]{1,0:T(8,128)(2,1)S(1)}, u32[]{:S(2)}, u32[]{:S(2)}) collective-permute-start(bf16[80,384]{1,0:T(8,128)(2,1)S(1)} %bitcast.142), channel_id=1, source_target_pairs={{0,4},{4,8},{8,12},{1,5},{5,9},{9,13},{2,6},{6,10},{10,14},{3,7},{... | collective-permute-start | bytes 184328 | tf_op jit(solution)/shard_map/ppermute | solution.py:23
  61.1 1.3 %collective-permute-start.4 = (bf16[80,384]{1,0:T(8,128)(2,1)S(1)}, bf16[80,384]{1,0:T(8,128)(2,1)S(1)}, u32[]{:S(2)}, u32[]{:S(2)}) collective-permute-start(bf16[80,384]{1,0:T(8,128)(2,1)S(1)} %bitcast.144), channel_id=1, source_target_pairs={{4,0},{8,4},{12,8},{5,1},{9,5},{13,9},{6,2},{10,6},{14,10},{7,3},{... | collective-permute-start | bytes 184328 | tf_op jit(solution)/shard_map/ppermute | solution.py:24
  62.5 4.4 %collective-permute-start.7 = (bf16[80,6]{0,1:T(8,128)(2,1)S(1)}, bf16[80,6]{0,1:T(8,128)(2,1)S(1)}, u32[]{:S(2)}, u32[]{:S(2)}) collective-permute-start(bf16[80,6]{0,1:T(8,128)(2,1)S(1)} %bitcast.154), channel_id=1, source_target_pairs={{0,1},{1,2},{2,3},{4,5},{5,6},{6,7},{8,9},{9,10},{10,11},{12,13},{... | collective-permute-start | bytes 2888 | tf_op jit(solution)/shard_map/ppermute | solution.py:25
  66.9 1.1 fusion.132
  68.2 1.9 %collective-permute-start.6 = (bf16[80,6]{0,1:T(8,128)(2,1)S(1)}, bf16[80,6]{0,1:T(8,128)(2,1)S(1)}, u32[]{:S(2)}, u32[]{:S(2)}) collective-permute-start(bf16[80,6]{0,1:T(8,128)(2,1)S(1)} %bitcast.156), channel_id=1, source_target_pairs={{1,0},{2,1},{3,2},{5,4},{6,5},{7,6},{9,8},{10,9},{11,10},{13,12},{... | collective-permute-start | bytes 2888 | tf_op jit(solution)/shard_map/ppermute | solution.py:26
  70.1 1.1 fusion.133
  71.5 1.0 copy.134
  72.5 0.6 collective-permute-done.6
  73.6 0.7 copy-done.13
  74.3 0.3 copy-done.7
  74.9 1.3 %fusion.146 = (bf16[80,2304]{1,0:T(8,128)(2,1)S(1)}, f32[80,2304]{1,0:T(8,128)S(1)}) fusion(f32[80,80]{1,0:T(8,128)S(1)} %copy-done, f32[80,2304]{1,0:T(8,128)S(1)} %fusion.148, f32[80,2304]{1,0:T(8,128)S(1)} %get-tuple-element.48, f32[80,1920]{1,0:T(8,128)S(1)} %copy-done.12, f32[80,384]{1,0:T(8,128)S(1)} %convert_element_type.84, ...), kind=kOutput, calls=%fused_computation.222 | convolution fusion | flops 180080640 | bytes 7052800 | tf_op jit(solution)/shard_map/dot_general | solution.py:73
  76.3 0.4 reshape.292
  77.0 4.9 %collective-permute-start.9 = (bf16[80,384]{1,0:T(8,128)(2,1)S(1)}, bf16[80,384]{1,0:T(8,128)(2,1)}, u32[]{:S(2)}, u32[]{:S(2)}) collective-permute-start(bf16[80,384]{1,0:T(8,128)(2,1)S(1)} %bitcast.143), channel_id=1, source_target_pairs={{0,4},{4,8},{8,12},{1,5},{5,9},{9,13},{2,6},{6,10},{10,14},{3,7},{... | collective-permute-start | bytes 184328 | tf_op jit(solution)/shard_map/ppermute | solution.py:23
  81.9 0.6 copy.150
  82.5 1.5 %collective-permute-start.8 = (bf16[80,384]{1,0:T(8,128)(2,1)}, bf16[80,384]{1,0:T(8,128)(2,1)}, u32[]{:S(2)}, u32[]{:S(2)}) collective-permute-start(bf16[80,384]{1,0:T(8,128)(2,1)} %bitcast.105), channel_id=1, source_target_pairs={{4,0},{8,4},{12,8},{5,1},{9,5},{13,9},{6,2},{10,6},{14,10},{7,3},{... | collective-permute-start | bytes 184328 | tf_op jit(solution)/shard_map/ppermute | solution.py:24
  84.2 3.3 %collective-permute-start.11 = (bf16[80,6]{0,1:T(8,128)(2,1)S(1)}, bf16[80,6]{0,1:T(8,128)(2,1)S(1)}, u32[]{:S(2)}, u32[]{:S(2)}) collective-permute-start(bf16[80,6]{0,1:T(8,128)(2,1)S(1)} %bitcast.155), channel_id=1, source_target_pairs={{0,1},{1,2},{2,3},{4,5},{5,6},{6,7},{8,9},{9,10},{10,11},{12,13},{... | collective-permute-start | bytes 2888 | tf_op jit(solution)/shard_map/ppermute | solution.py:25
  87.9 1.9 %collective-permute-start.10 = (bf16[80,6]{0,1:T(8,128)(2,1)S(1)}, bf16[80,6]{0,1:T(8,128)(2,1)S(1)}, u32[]{:S(2)}, u32[]{:S(2)}) collective-permute-start(bf16[80,6]{0,1:T(8,128)(2,1)S(1)} %bitcast.157), channel_id=1, source_target_pairs={{1,0},{2,1},{3,2},{5,4},{6,5},{7,6},{9,8},{10,9},{11,10},{13,12},{... | collective-permute-start | bytes 2888 | tf_op jit(solution)/shard_map/ppermute | solution.py:26
  89.9 1.1 fusion.131
  91.2 1.0 copy.136
  92.2 0.6 collective-permute-done.10
  93.3 0.9 convert_element_type.89
  94.2 0.8 convert_element_type.88
  95.1 1.3 %fusion.147 = (bf16[2304,80]{0,1:T(8,128)(2,1)S(1)}, f32[2304,80]{0,1:T(8,128)S(1)}) fusion(f32[80,80]{1,0:T(8,128)S(1)} %copy-done, f32[80,2304]{1,0:T(8,128)S(1)} %fusion.148, f32[80,2304]{1,0:T(8,128)S(1)} %get-tuple-element.50, f32[80,1920]{1,0:T(8,128)S(1)} %copy-done.10, f32[80,384]{1,0:T(8,128)S(1)} %convert_element_type.89, ...), kind=kOutput, calls=%fused_computation.223 | convolution fusion | flops 180080640 | bytes 7052800 | tf_op jit(solution)/shard_map/dot_general | solution.py:73
  96.5 1.2 %fusion.9 = f32[80,256]{1,0:T(8,128)S(1)} fusion(f32[80,256]{1,0:T(8,128)S(1)} %fusion.101, f32[2304,80]{0,1:T(8,128)S(1)} %get-tuple-element.52, pred[256,2304]{1,0:T(32,128)(4,1)S(1)} %copy-done.5), kind=kOutput, calls=%fused_computation.24 | convolution fusion | flops 566272000 | bytes 1490944 | tf_op jit(solution)/shard_map/dot_general | solution.py:149
  97.7 0.8 broadcast_select_fusion
  98.5 4.7 %all-to-all-start.2 = ((f32[80,4,256]{2,0,1:T(8,128)}), f32[80,4,256]{2,0,1:T(8,128)S(1)}, u32[]{:S(2)}, u32[]{:S(2)}) async-start(f32[80,4,256]{2,0,1:T(8,128)} %broadcast_select_fusion), calls=%async_computation.2 | async-start | bytes 655360 | tf_op jit(solution)/shard_map/all_to_all | solution.py:163
  103.2 0.8 copy.148
  103.9 8.7 %all-to-all-done.2 = f32[80,4,256]{2,0,1:T(8,128)S(1)} async-done(((f32[80,4,256]{2,0,1:T(8,128)}), f32[80,4,256]{2,0,1:T(8,128)S(1)}, u32[]{:S(2)}, u32[]{:S(2)}) %all-to-all-start.2) | async-done | bytes 327712 | tf_op jit(solution)/shard_map/all_to_all | solution.py:163
  112.9 6.3 %scatter_custom_fusion = f32[80,2048]{0,1:T(8,128)S(1)} fusion(s32[1024]{0:T(1024)S(1)} %bitcast.147, f32[1024,80]{1,0:T(8,128)S(1)} %copy.109, f32[]{:T(128)} %constant.109.clone.1), kind=kCustom, calls=%fused_computation.92 | custom fusion | flops 81920 | bytes 655364 | tf_op jit(solution)/shard_map/scatter-add | solution.py:164
  119.2 0.3 copy.110
  119.5 0.7 copy-done.3
  120.4 0.8 copy.137
  (132 shorter events, 6.6 us)
Async XLA Ops:
  0.6 33.1 %copy-start = (f32[80,80]{1,0:T(8,128)S(1)}, f32[80,80]{1,0:T(8,128)}, u32[]{:S(2)}) copy-start(f32[80,80]{1,0:T(8,128)} %param.16) | copy-start | bytes 76804
  0.6 10.2 %copy-start.15 = (bf16[80,6,384]{2,0,1:T(8,128)(2,1)S(1)}, bf16[80,6,384]{2,0,1:T(8,128)(2,1)}, u32[]{:S(2)}) copy-start(bf16[80,6,384]{2,0,1:T(8,128)(2,1)} %param.11) | copy-start | bytes 1105924
  0.7 10.3 %copy-start.14 = (bf16[80,8,256]{2,1,0:T(8,128)(2,1)S(1)}, bf16[80,8,256]{2,1,0:T(8,128)(2,1)}, u32[]{:S(2)}) copy-start(bf16[80,8,256]{2,1,0:T(8,128)(2,1)} %param.10) | copy-start | bytes 983044
  3.5 14.6 %copy-start.20 = (s32[1,1,256,1]{2,3,1,0:T(1,128)S(1)}, s32[1,1,256,1]{2,3,1,0:T(1,128)}, u32[]{:S(2)}) copy-start(s32[1,1,256,1]{2,3,1,0:T(1,128)} %param.17) | copy-start | bytes 3076
  3.5 14.6 %copy-start.21 = (s32[1,1,256]{2,1,0:T(1,128)S(1)}, s32[1,1,256]{2,1,0:T(1,128)}, u32[]{:S(2)}) copy-start(s32[1,1,256]{2,1,0:T(1,128)} %param.18) | copy-start | bytes 3076
  3.5 28.7 %collective-permute-start = (bf16[80,640]{1,0:T(8,128)(2,1)}, bf16[80,640]{1,0:T(8,128)(2,1)}, u32[]{:S(2)}, u32[]{:S(2)}) collective-permute-start(bf16[80,640]{1,0:T(8,128)(2,1)} %pad_maximum_fusion), channel_id=1, source_target_pairs={{4,0},{8,4},{12,8},{5,1},{9,5},{13,9},{6,2},{10,6},{14,10},{7,3},{... | collective-permute-start | bytes 307208 | tf_op jit(solution)/shard_map/ppermute | solution.py:24
  5.6 27.4 %collective-permute-start.1 = (bf16[80,640]{1,0:T(8,128)(2,1)}, bf16[80,640]{1,0:T(8,128)(2,1)}, u32[]{:S(2)}, u32[]{:S(2)}) collective-permute-start(bf16[80,640]{1,0:T(8,128)(2,1)} %pad_maximum_fusion.1), channel_id=1, source_target_pairs={{0,4},{4,8},{8,12},{1,5},{5,9},{9,13},{2,6},{6,10},{10,14},{3,7},{... | collective-permute-start | bytes 307208 | tf_op jit(solution)/shard_map/ppermute | solution.py:23
  11.4 18.1 %collective-permute-start.3 = (bf16[80,14]{0,1:T(8,128)(2,1)S(1)}, bf16[80,14]{0,1:T(8,128)(2,1)S(1)}, u32[]{:S(2)}, u32[]{:S(2)}) collective-permute-start(bf16[80,14]{0,1:T(8,128)(2,1)S(1)} %pad_maximum_fusion.3), channel_id=1, source_target_pairs={{0,1},{1,2},{2,3},{4,5},{5,6},{6,7},{8,9},{9,10},{10,11},{12,13},{... | collective-permute-start | bytes 6728 | tf_op jit(solution)/shard_map/ppermute | solution.py:25
  16.1 13.4 %collective-permute-start.2 = (bf16[80,14]{0,1:T(8,128)(2,1)S(1)}, bf16[80,14]{0,1:T(8,128)(2,1)S(1)}, u32[]{:S(2)}, u32[]{:S(2)}) collective-permute-start(bf16[80,14]{0,1:T(8,128)(2,1)S(1)} %pad_maximum_fusion.2), channel_id=1, source_target_pairs={{1,0},{2,1},{3,2},{5,4},{6,5},{7,6},{9,8},{10,9},{11,10},{13,12},{... | collective-permute-start | bytes 6728 | tf_op jit(solution)/shard_map/ppermute | solution.py:26
  18.7 13.4 %all-to-all-start = ((s32[4,256,1]{1,2,0:T(1,128)}), s32[4,256,1]{1,2,0:T(1,128)S(1)}, u32[]{:S(2)}, u32[]{:S(2)}) async-start(s32[4,256,1]{1,2,0:T(1,128)} %compare_select_fusion.1), calls=%async_computation | async-start | bytes 8192 | tf_op jit(solution)/shard_map/all_to_all | solution.py:120
  25.0 1.4 %copy-start.1 = (s32[24]{0:T(128)S(1)}, s32[24]{0:T(128)}, u32[]{:S(2)}) copy-start(s32[24]{0:T(128)} %param.19) | copy-start | bytes 292
  30.9 2.8 %copy-start.22 = (f32[80]{0:T(128)S(1)}, f32[80]{0:T(128)}, u32[]{:S(2)}) copy-start(f32[80]{0:T(128)} %param.12) | copy-start | bytes 964
  36.6 3.2 %copy-start.2 = (f32[80,2048]{1,0:T(8,128)}, f32[80,2048]{1,0:T(8,128)S(1)}, u32[]{:S(2)}) copy-start(f32[80,2048]{1,0:T(8,128)S(1)} %convolution_bitcast_fusion.2) | copy-start | bytes 1966084
  40.7 14.1 %all-to-all-start.1 = ((f32[80,4,256]{2,0,1:T(8,128)}), f32[80,4,256]{2,0,1:T(8,128)S(1)}, u32[]{:S(2)}, u32[]{:S(2)}) async-start(f32[80,4,256]{2,0,1:T(8,128)} %broadcast_select_fusion.1), calls=%async_computation.1 | async-start | bytes 655360 | tf_op jit(solution)/shard_map/all_to_all | solution.py:121
  46.8 8.0 %copy-start.4 = (pred[256,2304]{1,0:T(32,128)(4,1)S(1)}, pred[256,2304]{1,0:T(32,128)(4,1)}, u32[]{:S(2)}) copy-start(pred[256,2304]{1,0:T(32,128)(4,1)} %fusion.6) | copy-start | bytes 1769476
  49.3 6.4 %copy-start.6 = (f32[80,2303]{1,0:T(8,128)S(1)}, f32[80,2303]{1,0:T(8,128)}, u32[]{:S(2)}) copy-start(f32[80,2303]{1,0:T(8,128)} %get-tuple-element.21) | copy-start | bytes 2210884
  49.3 6.4 %copy-start.18 = (f32[80]{0:T(128)S(1)}, f32[80]{0:T(128)}, u32[]{:S(2)}) copy-start(f32[80]{0:T(128)} %param.14) | copy-start | bytes 964
  49.3 6.4 %copy-start.19 = (f32[80]{0:T(128)S(1)}, f32[80]{0:T(128)}, u32[]{:S(2)}) copy-start(f32[80]{0:T(128)} %param.13) | copy-start | bytes 964
  54.8 0.9 copy-start.16
  54.8 1.0 copy-start.17
  59.7 13.8 %collective-permute-start.5 = (bf16[80,384]{1,0:T(8,128)(2,1)S(1)}, bf16[80,384]{1,0:T(8,128)(2,1)S(1)}, u32[]{:S(2)}, u32[]{:S(2)}) collective-permute-start(bf16[80,384]{1,0:T(8,128)(2,1)S(1)} %bitcast.142), channel_id=1, source_target_pairs={{0,4},{4,8},{8,12},{1,5},{5,9},{9,13},{2,6},{6,10},{10,14},{3,7},{... | collective-permute-start | bytes 184328 | tf_op jit(solution)/shard_map/ppermute | solution.py:23
  61.1 12.5 %collective-permute-start.4 = (bf16[80,384]{1,0:T(8,128)(2,1)S(1)}, bf16[80,384]{1,0:T(8,128)(2,1)S(1)}, u32[]{:S(2)}, u32[]{:S(2)}) collective-permute-start(bf16[80,384]{1,0:T(8,128)(2,1)S(1)} %bitcast.144), channel_id=1, source_target_pairs={{4,0},{8,4},{12,8},{5,1},{9,5},{13,9},{6,2},{10,6},{14,10},{7,3},{... | collective-permute-start | bytes 184328 | tf_op jit(solution)/shard_map/ppermute | solution.py:24
  62.5 8.7 %collective-permute-start.7 = (bf16[80,6]{0,1:T(8,128)(2,1)S(1)}, bf16[80,6]{0,1:T(8,128)(2,1)S(1)}, u32[]{:S(2)}, u32[]{:S(2)}) collective-permute-start(bf16[80,6]{0,1:T(8,128)(2,1)S(1)} %bitcast.154), channel_id=1, source_target_pairs={{0,1},{1,2},{2,3},{4,5},{5,6},{6,7},{8,9},{9,10},{10,11},{12,13},{... | collective-permute-start | bytes 2888 | tf_op jit(solution)/shard_map/ppermute | solution.py:25
  68.2 4.9 %collective-permute-start.6 = (bf16[80,6]{0,1:T(8,128)(2,1)S(1)}, bf16[80,6]{0,1:T(8,128)(2,1)S(1)}, u32[]{:S(2)}, u32[]{:S(2)}) collective-permute-start(bf16[80,6]{0,1:T(8,128)(2,1)S(1)} %bitcast.156), channel_id=1, source_target_pairs={{1,0},{2,1},{3,2},{5,4},{6,5},{7,6},{9,8},{10,9},{11,10},{13,12},{... | collective-permute-start | bytes 2888 | tf_op jit(solution)/shard_map/ppermute | solution.py:26
  73.2 1.1 copy-start.13
  73.4 1.2 copy-start.7
  73.4 1.4 %copy-start.9 = (f32[10,8,6,384]{3,1,2,0:T(8,128)S(1)}, f32[10,8,6,384]{3,1,2,0:T(8,128)}, u32[]{:S(2)}) copy-start(f32[10,8,6,384]{3,1,2,0:T(8,128)} %copy.134) | copy-start | bytes 2211844
  73.4 1.6 %copy-start.12 = (f32[80,1920]{1,0:T(8,128)S(1)}, f32[80,1920]{1,0:T(8,128)}, u32[]{:S(2)}) copy-start(f32[80,1920]{1,0:T(8,128)} %get-tuple-element.19) | copy-start | bytes 1843204
  77.0 16.3 %collective-permute-start.9 = (bf16[80,384]{1,0:T(8,128)(2,1)S(1)}, bf16[80,384]{1,0:T(8,128)(2,1)}, u32[]{:S(2)}, u32[]{:S(2)}) collective-permute-start(bf16[80,384]{1,0:T(8,128)(2,1)S(1)} %bitcast.143), channel_id=1, source_target_pairs={{0,4},{4,8},{8,12},{1,5},{5,9},{9,13},{2,6},{6,10},{10,14},{3,7},{... | collective-permute-start | bytes 184328 | tf_op jit(solution)/shard_map/ppermute | solution.py:23
  82.5 11.7 %collective-permute-start.8 = (bf16[80,384]{1,0:T(8,128)(2,1)}, bf16[80,384]{1,0:T(8,128)(2,1)}, u32[]{:S(2)}, u32[]{:S(2)}) collective-permute-start(bf16[80,384]{1,0:T(8,128)(2,1)} %bitcast.105), channel_id=1, source_target_pairs={{4,0},{8,4},{12,8},{5,1},{9,5},{13,9},{6,2},{10,6},{14,10},{7,3},{... | collective-permute-start | bytes 184328 | tf_op jit(solution)/shard_map/ppermute | solution.py:24
  84.2 6.8 %collective-permute-start.11 = (bf16[80,6]{0,1:T(8,128)(2,1)S(1)}, bf16[80,6]{0,1:T(8,128)(2,1)S(1)}, u32[]{:S(2)}, u32[]{:S(2)}) collective-permute-start(bf16[80,6]{0,1:T(8,128)(2,1)S(1)} %bitcast.155), channel_id=1, source_target_pairs={{0,1},{1,2},{2,3},{4,5},{5,6},{6,7},{8,9},{9,10},{10,11},{12,13},{... | collective-permute-start | bytes 2888 | tf_op jit(solution)/shard_map/ppermute | solution.py:25
  87.9 4.9 %collective-permute-start.10 = (bf16[80,6]{0,1:T(8,128)(2,1)S(1)}, bf16[80,6]{0,1:T(8,128)(2,1)S(1)}, u32[]{:S(2)}, u32[]{:S(2)}) collective-permute-start(bf16[80,6]{0,1:T(8,128)(2,1)S(1)} %bitcast.157), channel_id=1, source_target_pairs={{1,0},{2,1},{3,2},{5,4},{6,5},{7,6},{9,8},{10,9},{11,10},{13,12},{... | collective-permute-start | bytes 2888 | tf_op jit(solution)/shard_map/ppermute | solution.py:26
  93.1 2.0 %copy-start.8 = (f32[10,8,6,384]{3,1,2,0:T(8,128)S(1)}, f32[10,8,6,384]{3,1,2,0:T(8,128)}, u32[]{:S(2)}) copy-start(f32[10,8,6,384]{3,1,2,0:T(8,128)} %copy.136) | copy-start | bytes 2211844
  93.1 2.0 %copy-start.10 = (f32[80,1920]{1,0:T(8,128)S(1)}, f32[80,1920]{1,0:T(8,128)}, u32[]{:S(2)}) copy-start(f32[80,1920]{1,0:T(8,128)} %get-tuple-element.15) | copy-start | bytes 1843204
  93.1 2.0 %copy-start.11 = (f32[80,1920]{1,0:T(8,128)S(1)}, f32[80,1920]{1,0:T(8,128)}, u32[]{:S(2)}) copy-start(f32[80,1920]{1,0:T(8,128)} %get-tuple-element.16) | copy-start | bytes 1843204
  95.1 1.4 %copy-start.5 = (pred[256,2304]{1,0:T(32,128)(4,1)S(1)}, pred[256,2304]{1,0:T(32,128)(4,1)}, u32[]{:S(2)}) copy-start(pred[256,2304]{1,0:T(32,128)(4,1)} %fusion.6) | copy-start | bytes 1769476
  98.5 14.2 %all-to-all-start.2 = ((f32[80,4,256]{2,0,1:T(8,128)}), f32[80,4,256]{2,0,1:T(8,128)S(1)}, u32[]{:S(2)}, u32[]{:S(2)}) async-start(f32[80,4,256]{2,0,1:T(8,128)} %broadcast_select_fusion), calls=%async_computation.2 | async-start | bytes 655360 | tf_op jit(solution)/shard_map/all_to_all | solution.py:163
  119.2 1.1 copy-start.3
  119.2 1.1 copy-start.23
where the time goes:
time: 122 us; the launch traced here: 121 us
  starting transfers between devices  46.3 us (38%)
  local copies, waits for them, and re-layouts  30.1 us (25%)
  other arithmetic  18.7 us (15%)
  waiting for transfers between devices  13.9 us (11%)
  matrix products  10.8 us (9%)
  between operations  1.45 us (1%)
    ppermute x3, starting transfers between devices, exchange(): left = lax.ppermute(last_cols, Y_AXES, fwd_y)  12.1 us
    ppermute x3, starting transfers between devices, exchange(): above = lax.ppermute(last_rows, 'gx', fwd_x)  11.5 us
    unnamed x68, local copies, waits for them, and re-layouts  10.8 us
    all_to_all x1, waiting for transfers between devices, body(): lax.all_to_all(outgoing, 'gx', split_axis=1, concat_axis=1, tiled=True)  8.71 us
    dot_general x4, matrix products, mix_levels(): jnp.dot(matrix, flat, precision=HI, preferred_element_type=jnp.float32)  8.71 us
    convert_element_type x12, other arithmetic, flat_stencil(): above, below, left, right = (h.astype(flat.dtype) for h in halo)  6.43 us
    scatter-add x1, other arithmetic, body(): summed = jnp.zeros_like(flat_parent).at[:, served_ids].add(incoming)  6.28 us
    ppermute x3, starting transfers between devices, exchange(): right = lax.ppermute(first_cols, Y_AXES, bwd_y)  5.74 us
  transfers between devices with their start and end apart: 15, of which 4 were waited for; matrix products, arithmetic and copies ran while one was open for 23% of the time, Pallas kernels for 0%

commit v1 on v0

--- a/solution.py
+++ b/solution.py
@@ -5,6 +5,18 @@
 
 Y_AXES = ("gy", "gz")
 HI = lax.Precision.HIGHEST
+
+
+def in_blocks(shard, dim, length):
+    shape = shard.shape
+    parts = shard.reshape(*shape[:dim], length, shape[dim] // length, *shape[dim + 1 :])
+    return jnp.moveaxis(parts, dim, 0)
+
+
+def joined_along(parts, dim):
+    shape = list(parts.shape[1:])
+    shape[dim] *= parts.shape[0]
+    return jnp.moveaxis(parts, 0, dim).reshape(shape)
 
 
 def shift_pairs(count):
@@ -118,9 +130,15 @@
         places = owners * slots + order_in
         wanted = jnp.zeros((tiles_x * slots,), jnp.int32).at[places].set(cells)
     served_ids = lax.all_to_all(wanted, "gx", split_axis=0, concat_axis=0, tiled=True)
-    answers = lax.all_to_all(
-        jnp.take(flat_parent, served_ids, axis=1), "gx", split_axis=1, concat_axis=1, tiled=True
-    )
+    x = jnp.take(flat_parent, served_ids, axis=1)
+    devices, index = (lax.axis_size("gx"), lax.axis_index("gx"))
+    pieces = in_blocks(x, 1, devices)
+    outs = [pieces[index]]
+    for step in range(1, devices):
+        sent = pieces[index ^ step]
+        outs.append(lax.ppermute(sent, "gx", [(i_2, i_2 ^ step) for i_2 in range(devices)]))
+    pieces = jnp.stack(outs)[index ^ jnp.arange(devices)]
+    answers = joined_along(pieces, 1)
     if slots >= requests:
         answers = answers.reshape(levels, tiles_x, slots)[:, :, :requests]
         forcing_flat = answers[:, 0, :]

time: 122 us -> 118 us (0.967)
  other arithmetic: 18.7 us -> 11.8 us
  local copies, waits for them, and re-layouts: 30.1 us -> 32.6 us
    convert_element_type x12, other arithmetic: 6.43 us -> 1.39 us  [flat_stencil(): above, below, left, right = (h.astype(flat.dtype) for h in halo)]
    all_to_all x1 -> x0, starting transfers between devices: 4.54 us -> none  [body(): lax.all_to_all(jnp.take(flat_parent, served_ids, axis=1), 'gx', split_axi...]
    all_to_all x1 -> x0, waiting for transfers between devices: 3.94 us -> none  [body(): lax.all_to_all(jnp.take(flat_parent, served_ids, axis=1), 'gx', split_axi...]
    ppermute x0 -> x3, starting transfers between devices: none -> 3.76 us  [body(): lax.ppermute(sent, 'gx', [(i_2, i_2 ^ step) for i_2 in range(devices)])]
    ppermute x0 -> x3, waiting for transfers between devices: none -> 3.65 us  [body(): lax.ppermute(sent, 'gx', [(i_2, i_2 ^ step) for i_2 in range(devices)])]
    ppermute x3, starting transfers between devices: 5.74 us -> 8.84 us  [exchange(): right = lax.ppermute(first_cols, Y_AXES, bwd_y)]
    slice x6, local copies, waits for them, and re-layouts: 0.79 us -> 2.83 us  [exchange(): first_cols = jnp.concatenate([b[:, :, 0] for b in blocks], axis=1)]
    all_to_all x1, starting transfers between devices: 3.58 us -> 5.38 us  [body(): lax.all_to_all(wanted, 'gx', split_axis=0, concat_axis=0, tiled=True)]
  transfers between devices with their start and end apart: 15 -> 17, of which waited for: 4 -> 3; matrix products, arithmetic and copies ran while one was open for 23% -> 20% of each run, Pallas kernels for 0% -> 0%
where the time goes in v1:
time: 118 us; the launch traced here: 117 us
  starting transfers between devices  47 us (40%)
  local copies, waits for them, and re-layouts  32.6 us (28%)
  waiting for transfers between devices  13.3 us (11%)
  other arithmetic  11.8 us (10%)
  matrix products  10.3 us (9%)
  between operations  1.66 us (1%)
    unnamed x80, local copies, waits for them, and re-layouts  12.5 us
    ppermute x3, starting transfers between devices, exchange(): above = lax.ppermute(last_rows, 'gx', fwd_x)  11.4 us
    ppermute x3, starting transfers between devices, exchange(): left = lax.ppermute(last_cols, Y_AXES, fwd_y)  10.3 us
    all_to_all x1, waiting for transfers between devices, body(): lax.all_to_all(outgoing, 'gx', split_axis=1, concat_axis=1, tiled=True)  9.6 us
    ppermute x3, starting transfers between devices, exchange(): right = lax.ppermute(first_cols, Y_AXES, bwd_y)  8.84 us
    dot_general x4, matrix products, mix_levels(): jnp.dot(matrix, flat, precision=HI, preferred_element_type=jnp.float32)  8.25 us
    scatter-add x1, other arithmetic, body(): summed = jnp.zeros_like(flat_parent).at[:, served_ids].add(incoming)  6.28 us
    all_to_all x1, starting transfers between devices, body(): lax.all_to_all(wanted, 'gx', split_axis=0, concat_axis=0, tiled=True)  5.38 us
  transfers between devices with their start and end apart: 17, of which 3 were waited for; matrix products, arithmetic and copies ran while one was open for 20% of the time, Pallas kernels for 0%

profile of v1, /device:TPU:1, one launch (start us, length us, event | category | flops | bytes accessed | tf_op | source)
XLA Modules:
  0.0 116.8 jit_solution(15939586031200092001)
XLA Ops:
  0.7 1.2 %fusion.144 = (bf16[80,8,1]{2,1,0:T(8,128)(2,1)S(1)}, bf16[80,8,1]{2,1,0:T(8,128)(2,1)S(1)}) fusion(bf16[80,8,256]{2,1,0:T(8,128)(2,1)} %param.10), kind=kLoop, calls=%fused_computation.228 | loop fusion | bytes 5120 | tf_op jit(solution)/shard_map/slice | solution.py:34
  2.0 1.1 fusion.143
  3.3 1.9 %collective-permute-start.2 = (bf16[80,14]{0,1:T(8,128)(2,1)S(1)}, bf16[80,14]{0,1:T(8,128)(2,1)S(1)}, u32[]{:S(2)}, u32[]{:S(2)}) collective-permute-start(bf16[80,14]{0,1:T(8,128)(2,1)S(1)} %pad_maximum_fusion.3), channel_id=1, source_target_pairs={{1,0},{2,1},{3,2},{5,4},{6,5},{7,6},{9,8},{10,9},{11,10},{13,12},{... | collective-permute-start | bytes 6728 | tf_op jit(solution)/shard_map/ppermute | solution.py:38
  5.5 4.5 %collective-permute-start.3 = (bf16[80,14]{0,1:T(8,128)(2,1)S(1)}, bf16[80,14]{0,1:T(8,128)(2,1)S(1)}, u32[]{:S(2)}, u32[]{:S(2)}) collective-permute-start(bf16[80,14]{0,1:T(8,128)(2,1)S(1)} %pad_maximum_fusion.4), channel_id=1, source_target_pairs={{0,1},{1,2},{2,3},{4,5},{5,6},{6,7},{8,9},{9,10},{10,11},{12,13},{... | collective-permute-start | bytes 6728 | tf_op jit(solution)/shard_map/ppermute | solution.py:37
  10.2 3.2 %collective-permute-start.1 = (bf16[80,640]{1,0:T(8,128)(2,1)S(1)}, bf16[80,640]{1,0:T(8,128)(2,1)S(1)}, u32[]{:S(2)}, u32[]{:S(2)}) collective-permute-start(bf16[80,640]{1,0:T(8,128)(2,1)S(1)} %pad_maximum_fusion.2), channel_id=1, source_target_pairs={{0,4},{4,8},{8,12},{1,5},{5,9},{9,13},{2,6},{6,10},{10,14},{3,7},{... | collective-permute-start | bytes 307208 | tf_op jit(solution)/shard_map/ppermute | solution.py:35
  13.5 1.3 %collective-permute-start = (bf16[80,640]{1,0:T(8,128)(2,1)S(1)}, bf16[80,640]{1,0:T(8,128)(2,1)S(1)}, u32[]{:S(2)}, u32[]{:S(2)}) collective-permute-start(bf16[80,640]{1,0:T(8,128)(2,1)S(1)} %pad_maximum_fusion.1), channel_id=1, source_target_pairs={{4,0},{8,4},{12,8},{5,1},{9,5},{13,9},{6,2},{10,6},{14,10},{7,3},{... | collective-permute-start | bytes 307208 | tf_op jit(solution)/shard_map/ppermute | solution.py:36
  14.8 0.6 compare_select_fusion.1
  15.4 5.4 %all-to-all-start = ((s32[4,256,1]{1,2,0:T(1,128)}), s32[4,256,1]{1,2,0:T(1,128)S(1)}, u32[]{:S(2)}, u32[]{:S(2)}) async-start(s32[4,256,1]{1,2,0:T(1,128)} %compare_select_fusion.1), calls=%async_computation | async-start | bytes 8192 | tf_op jit(solution)/shard_map/all_to_all | solution.py:132
  20.8 0.2 fusion.137
  21.1 1.1 fusion.138
  22.4 1.4 %fusion.135 = (f32[80,2303]{1,0:T(8,128)}, f32[80,2303]{1,0:T(8,128)}) fusion(f32[80,2304]{1,0:T(8,128)S(1)} %bitcast.120), kind=kLoop, calls=%fused_computation.219 | loop fusion | bytes 2947840 | tf_op jit(solution)/shard_map/slice | solution.py:76
  23.8 1.2 fusion.136
  25.0 0.6 gather_fusion
  25.8 2.2 %fusion.6 = pred[256,2304]{1,0:T(32,128)(4,1)} fusion(s32[256]{0:T(256)S(1)} %get-tuple-element.62, s32[256]{0:T(256)S(1)} %get-tuple-element.63, s32[2304]{0:T(1024)S(1)} %get-tuple-element.66, s32[2304]{0:T(1024)S(1)} %get-tuple-element.67, s32[256]{0:T(256)S(1)} %get-tuple-element.61, s32[256]{0:T(256)S(1)} %get-tuple-element.64, ...), kind=kLoop, calls=%fused_computation.21 | loop fusion | flops 13565952 | bytes 635904 | tf_op jit(solution)/shard_map/and | solution.py:103
  28.4 1.0 copy.133
  29.6 1.0 copy.134
  30.9 1.0 copy.135
  32.2 1.0 copy.136
  33.3 0.6 copy-done.20
  33.9 2.8 %convolution_bitcast_fusion.2 = f32[80,2048]{1,0:T(8,128)S(1)} fusion(f32[80,80]{1,0:T(8,128)S(1)} %copy-done, f32[80,2048]{1,0:T(8,128)S(1)} %bitcast.125, f32[80,256]{1,0:T(8,128)S(1)} %slice_convert_fusion.3, f32[80,1792]{1,0:T(8,128)} %get-tuple-element.28, f32[80,1792]{1,0:T(8,128)} %get-tuple-element.27, f32[80,256]{1,0:T(8,128)S(1)} %slice_convert_fusion.2, ...), kind=kOutput, calls=%fused_computation.14 | convolution fusion | flops 159088640 | bytes 5272256 | tf_op jit(solution)/shard_map/dot_general | solution.py:85
  36.7 0.3 copy.97
  37.1 2.8 %gather_fusion.1 = f32[1024,80]{1,0:T(8,128)S(1)} fusion(f32[80,2048]{0,1:T(8,128)S(1)} %copy.97, s32[1024]{0:T(1024)S(1)} %broadcast_clamp_fusion), kind=kCustom, calls=%fused_computation.1 | custom fusion | bytes 659456 | tf_op jit(solution)/shard_map/jit(_take)/gather | solution.py:133
  40.3 1.5 %collective-permute-start.4 = (f32[80,256]{1,0:T(8,128)S(1)}, f32[80,256]{1,0:T(8,128)S(1)}, u32[]{:S(2)}, u32[]{:S(2)}) collective-permute-start(f32[80,256]{1,0:T(8,128)S(1)} %bitcast.157), channel_id=1, source_target_pairs={{0,4},{4,0},{8,12},{12,8},{1,5},{5,1},{9,13},{13,9},{2,6},{6,2},{1... | collective-permute-start | bytes 245768 | tf_op jit(solution)/shard_map/ppermute | solution.py:139
  41.9 2.1 %collective-permute-start.5 = (f32[80,256]{1,0:T(8,128)S(1)}, f32[80,256]{1,0:T(8,128)S(1)}, u32[]{:S(2)}, u32[]{:S(2)}) collective-permute-start(f32[80,256]{1,0:T(8,128)S(1)} %bitcast.158), channel_id=1, source_target_pairs={{0,8},{4,12},{8,0},{12,4},{1,9},{5,13},{9,1},{13,5},{2,10},{6,14},... | collective-permute-start | bytes 245768 | tf_op jit(solution)/shard_map/ppermute | solution.py:139
  44.2 0.7 slice_convert_fusion
  44.9 0.7 slice_convert_fusion.1
  45.7 1.5 %collective-permute-done.5 = f32[80,256]{1,0:T(8,128)S(1)} collective-permute-done((f32[80,256]{1,0:T(8,128)S(1)}, f32[80,256]{1,0:T(8,128)S(1)}, u32[]{:S(2)}, u32[]{:S(2)}) %collective-permute-start.5) | collective-permute-done | bytes 81952 | tf_op jit(solution)/shard_map/ppermute | solution.py:139
  47.2 2.1 %collective-permute-done.6 = f32[80,256]{1,0:T(8,128)S(1)} collective-permute-done((f32[80,256]{1,0:T(8,128)S(1)}, f32[80,256]{1,0:T(8,128)S(1)}, u32[]{:S(2)}, u32[]{:S(2)}) %collective-permute-start.6) | collective-permute-done | bytes 81952 | tf_op jit(solution)/shard_map/ppermute | solution.py:139
  49.3 0.6 gather_fusion.2
  50.0 0.8 fusion.149
  50.9 0.2 copy-done.6
  51.1 0.2 copy-done.7
  51.4 2.8 %fusion.146 = (bf16[80,2304]{1,0:T(8,128)(2,1)S(1)}, f32[80,2304]{1,0:T(8,128)S(1)}) fusion(f32[80,80]{1,0:T(8,128)S(1)} %copy-done, f32[80,2304]{1,0:T(8,128)S(1)} %fusion.149, f32[80,2304]{1,0:T(8,128)S(1)} %bitcast.122, f32[80,1920]{1,0:T(8,128)} %get-tuple-element.23, f32[80,384]{1,0:T(8,128)S(1)} %copy-done.18, f32[80,384]{1,0:T(8,128)S(1)} %copy-done.19, ...), kind=kOutput, calls=%fused_computation.230 | convolution fusion | flops 180080640 | bytes 7052800 | tf_op jit(solution)/shard_map/dot_general | solution.py:85
  54.2 0.4 reshape.309
  55.1 4.6 %collective-permute-start.9 = (bf16[80,6]{0,1:T(8,128)(2,1)S(1)}, bf16[80,6]{0,1:T(8,128)(2,1)S(1)}, u32[]{:S(2)}, u32[]{:S(2)}) collective-permute-start(bf16[80,6]{0,1:T(8,128)(2,1)S(1)} %bitcast.175), channel_id=1, source_target_pairs={{1,0},{2,1},{3,2},{5,4},{6,5},{7,6},{9,8},{10,9},{11,10},{13,12},{... | collective-permute-start | bytes 2888 | tf_op jit(solution)/shard_map/ppermute | solution.py:38
  59.9 2.6 %collective-permute-start.10 = (bf16[80,6]{0,1:T(8,128)(2,1)S(1)}, bf16[80,6]{0,1:T(8,128)(2,1)S(1)}, u32[]{:S(2)}, u32[]{:S(2)}) collective-permute-start(bf16[80,6]{0,1:T(8,128)(2,1)S(1)} %bitcast.173), channel_id=1, source_target_pairs={{0,1},{1,2},{2,3},{4,5},{5,6},{6,7},{8,9},{9,10},{10,11},{12,13},{... | collective-permute-start | bytes 2888 | tf_op jit(solution)/shard_map/ppermute | solution.py:37
  62.5 1.1 fusion.133
  63.6 1.3 %collective-permute-start.7 = (bf16[80,384]{1,0:T(8,128)(2,1)S(1)}, bf16[80,384]{1,0:T(8,128)(2,1)S(1)}, u32[]{:S(2)}, u32[]{:S(2)}) collective-permute-start(bf16[80,384]{1,0:T(8,128)(2,1)S(1)} %bitcast.160), channel_id=1, source_target_pairs={{4,0},{8,4},{12,8},{5,1},{9,5},{13,9},{6,2},{10,6},{14,10},{7,3},{... | collective-permute-start | bytes 184328 | tf_op jit(solution)/shard_map/ppermute | solution.py:36
  64.9 4.2 %collective-permute-start.8 = (bf16[80,384]{1,0:T(8,128)(2,1)S(1)}, bf16[80,384]{1,0:T(8,128)(2,1)S(1)}, u32[]{:S(2)}, u32[]{:S(2)}) collective-permute-start(bf16[80,384]{1,0:T(8,128)(2,1)S(1)} %bitcast.162), channel_id=1, source_target_pairs={{0,4},{4,8},{8,12},{1,5},{5,9},{9,13},{2,6},{6,10},{10,14},{3,7},{... | collective-permute-start | bytes 184328 | tf_op jit(solution)/shard_map/ppermute | solution.py:35
  69.1 1.1 fusion.134
  70.5 1.0 copy.137
  72.0 0.7 copy-done.15
  72.7 0.3 copy-done.9
  72.9 0.2 copy-done.11
  73.3 1.3 %fusion.147 = (bf16[80,2304]{1,0:T(8,128)(2,1)S(1)}, f32[80,2304]{1,0:T(8,128)S(1)}) fusion(f32[80,80]{1,0:T(8,128)S(1)} %copy-done, f32[80,2304]{1,0:T(8,128)S(1)} %fusion.149, f32[80,2304]{1,0:T(8,128)S(1)} %get-tuple-element.52, f32[80,1920]{1,0:T(8,128)S(1)} %copy-done.14, f32[80,384]{1,0:T(8,128)S(1)} %convert_element_type.84, ...), kind=kOutput, calls=%fused_computation.231 | convolution fusion | flops 180080640 | bytes 7052800 | tf_op jit(solution)/shard_map/dot_general | solution.py:85
  74.7 0.4 reshape.312
  75.6 2.3 %collective-permute-start.13 = (bf16[80,6]{0,1:T(8,128)(2,1)S(1)}, bf16[80,6]{0,1:T(8,128)(2,1)S(1)}, u32[]{:S(2)}, u32[]{:S(2)}) collective-permute-start(bf16[80,6]{0,1:T(8,128)(2,1)S(1)} %bitcast.176), channel_id=1, source_target_pairs={{1,0},{2,1},{3,2},{5,4},{6,5},{7,6},{9,8},{10,9},{11,10},{13,12},{... | collective-permute-start | bytes 2888 | tf_op jit(solution)/shard_map/ppermute | solution.py:38
  78.0 3.3 %collective-permute-start.14 = (bf16[80,6]{0,1:T(8,128)(2,1)S(1)}, bf16[80,6]{0,1:T(8,128)(2,1)S(1)}, u32[]{:S(2)}, u32[]{:S(2)}) collective-permute-start(bf16[80,6]{0,1:T(8,128)(2,1)S(1)} %bitcast.174), channel_id=1, source_target_pairs={{0,1},{1,2},{2,3},{4,5},{5,6},{6,7},{8,9},{9,10},{10,11},{12,13},{... | collective-permute-start | bytes 2888 | tf_op jit(solution)/shard_map/ppermute | solution.py:37
  81.3 0.3 fusion.131
  81.6 1.3 %collective-permute-start.11 = (bf16[80,384]{1,0:T(8,128)(2,1)S(1)}, bf16[80,384]{1,0:T(8,128)(2,1)S(1)}, u32[]{:S(2)}, u32[]{:S(2)}) collective-permute-start(bf16[80,384]{1,0:T(8,128)(2,1)S(1)} %bitcast.161), channel_id=1, source_target_pairs={{4,0},{8,4},{12,8},{5,1},{9,5},{13,9},{6,2},{10,6},{14,10},{7,3},{... | collective-permute-start | bytes 184328 | tf_op jit(solution)/shard_map/ppermute | solution.py:36
  82.9 4.0 %collective-permute-start.12 = (bf16[80,384]{1,0:T(8,128)(2,1)S(1)}, bf16[80,384]{1,0:T(8,128)(2,1)S(1)}, u32[]{:S(2)}, u32[]{:S(2)}) collective-permute-start(bf16[80,384]{1,0:T(8,128)(2,1)S(1)} %bitcast.163), channel_id=1, source_target_pairs={{0,4},{4,8},{8,12},{1,5},{5,9},{9,13},{2,6},{6,10},{10,14},{3,7},{... | collective-permute-start | bytes 184328 | tf_op jit(solution)/shard_map/ppermute | solution.py:35
  86.9 1.1 fusion.132
  88.3 1.0 copy.139
  89.8 0.9 copy-done.10
  91.0 1.3 %fusion.148 = (bf16[2304,80]{0,1:T(8,128)(2,1)S(1)}, f32[2304,80]{0,1:T(8,128)S(1)}) fusion(f32[80,80]{1,0:T(8,128)S(1)} %copy-done, f32[80,2304]{1,0:T(8,128)S(1)} %fusion.149, f32[80,2304]{1,0:T(8,128)S(1)} %get-tuple-element.54, f32[80,1920]{1,0:T(8,128)S(1)} %copy-done.12, f32[80,384]{1,0:T(8,128)S(1)} %convert_element_type.89, ...), kind=kOutput, calls=%fused_computation.232 | convolution fusion | flops 180080640 | bytes 7052800 | tf_op jit(solution)/shard_map/dot_general | solution.py:85
  92.4 1.2 %fusion.9 = f32[80,256]{1,0:T(8,128)S(1)} fusion(f32[80,256]{1,0:T(8,128)S(1)} %fusion.101, f32[2304,80]{0,1:T(8,128)S(1)} %get-tuple-element.56, pred[256,2304]{1,0:T(32,128)(4,1)S(1)} %copy-done.5), kind=kOutput, calls=%fused_computation.25 | convolution fusion | flops 566272000 | bytes 1490944 | tf_op jit(solution)/shard_map/dot_general | solution.py:167
  93.6 0.8 broadcast_select_fusion.1
  94.4 3.5 %all-to-all-start.1 = ((f32[80,4,256]{2,0,1:T(8,128)}), f32[80,4,256]{2,0,1:T(8,128)S(1)}, u32[]{:S(2)}, u32[]{:S(2)}) async-start(f32[80,4,256]{2,0,1:T(8,128)} %broadcast_select_fusion.1), calls=%async_computation.1 | async-start | bytes 655360 | tf_op jit(solution)/shard_map/all_to_all | solution.py:181
  97.9 0.8 copy.152
  98.6 9.6 %all-to-all-done.1 = f32[80,4,256]{2,0,1:T(8,128)S(1)} async-done(((f32[80,4,256]{2,0,1:T(8,128)}), f32[80,4,256]{2,0,1:T(8,128)S(1)}, u32[]{:S(2)}, u32[]{:S(2)}) %all-to-all-start.1) | async-done | bytes 327712 | tf_op jit(solution)/shard_map/all_to_all | solution.py:181
  108.5 6.3 %scatter_custom_fusion = f32[80,2048]{0,1:T(8,128)S(1)} fusion(s32[1024]{0:T(1024)S(1)} %bitcast.166, f32[1024,80]{1,0:T(8,128)S(1)} %copy.115, f32[]{:T(128)} %constant.113.clone.1), kind=kCustom, calls=%fused_computation.93 | custom fusion | flops 81920 | bytes 655364 | tf_op jit(solution)/shard_map/scatter-add | solution.py:182
  114.8 0.3 copy.116
  115.1 0.7 copy-done.3
  116.0 0.8 copy.141
  (156 shorter events, 6.8 us)
Async XLA Ops:
  0.6 33.3 %copy-start = (f32[80,80]{1,0:T(8,128)S(1)}, f32[80,80]{1,0:T(8,128)}, u32[]{:S(2)}) copy-start(f32[80,80]{1,0:T(8,128)} %param.16) | copy-start | bytes 76804
  0.6 9.4 %copy-start.16 = (bf16[80,8,256]{2,1,0:T(8,128)(2,1)S(1)}, bf16[80,8,256]{2,1,0:T(8,128)(2,1)}, u32[]{:S(2)}) copy-start(bf16[80,8,256]{2,1,0:T(8,128)(2,1)} %param.10) | copy-start | bytes 983044
  0.7 9.5 %copy-start.17 = (bf16[80,6,384]{2,0,1:T(8,128)(2,1)S(1)}, bf16[80,6,384]{2,0,1:T(8,128)(2,1)}, u32[]{:S(2)}) copy-start(bf16[80,6,384]{2,0,1:T(8,128)(2,1)} %param.11) | copy-start | bytes 1105924
  2.0 12.7 %copy-start.26 = (s32[1,1,256,1]{2,3,1,0:T(1,128)S(1)}, s32[1,1,256,1]{2,3,1,0:T(1,128)}, u32[]{:S(2)}) copy-start(s32[1,1,256,1]{2,3,1,0:T(1,128)} %param.17) | copy-start | bytes 3076
  2.0 12.8 %copy-start.27 = (s32[1,1,256]{2,1,0:T(1,128)S(1)}, s32[1,1,256]{2,1,0:T(1,128)}, u32[]{:S(2)}) copy-start(s32[1,1,256]{2,1,0:T(1,128)} %param.18) | copy-start | bytes 3076
  3.3 24.8 %collective-permute-start.2 = (bf16[80,14]{0,1:T(8,128)(2,1)S(1)}, bf16[80,14]{0,1:T(8,128)(2,1)S(1)}, u32[]{:S(2)}, u32[]{:S(2)}) collective-permute-start(bf16[80,14]{0,1:T(8,128)(2,1)S(1)} %pad_maximum_fusion.3), channel_id=1, source_target_pairs={{1,0},{2,1},{3,2},{5,4},{6,5},{7,6},{9,8},{10,9},{11,10},{13,12},{... | collective-permute-start | bytes 6728 | tf_op jit(solution)/shard_map/ppermute | solution.py:38
  5.5 22.6 %collective-permute-start.3 = (bf16[80,14]{0,1:T(8,128)(2,1)S(1)}, bf16[80,14]{0,1:T(8,128)(2,1)S(1)}, u32[]{:S(2)}, u32[]{:S(2)}) collective-permute-start(bf16[80,14]{0,1:T(8,128)(2,1)S(1)} %pad_maximum_fusion.4), channel_id=1, source_target_pairs={{0,1},{1,2},{2,3},{4,5},{5,6},{6,7},{8,9},{9,10},{10,11},{12,13},{... | collective-permute-start | bytes 6728 | tf_op jit(solution)/shard_map/ppermute | solution.py:37
  10.2 23.0 %collective-permute-start.1 = (bf16[80,640]{1,0:T(8,128)(2,1)S(1)}, bf16[80,640]{1,0:T(8,128)(2,1)S(1)}, u32[]{:S(2)}, u32[]{:S(2)}) collective-permute-start(bf16[80,640]{1,0:T(8,128)(2,1)S(1)} %pad_maximum_fusion.2), channel_id=1, source_target_pairs={{0,4},{4,8},{8,12},{1,5},{5,9},{9,13},{2,6},{6,10},{10,14},{3,7},{... | collective-permute-start | bytes 307208 | tf_op jit(solution)/shard_map/ppermute | solution.py:35
  13.5 19.8 %collective-permute-start = (bf16[80,640]{1,0:T(8,128)(2,1)S(1)}, bf16[80,640]{1,0:T(8,128)(2,1)S(1)}, u32[]{:S(2)}, u32[]{:S(2)}) collective-permute-start(bf16[80,640]{1,0:T(8,128)(2,1)S(1)} %pad_maximum_fusion.1), channel_id=1, source_target_pairs={{4,0},{8,4},{12,8},{5,1},{9,5},{13,9},{6,2},{10,6},{14,10},{7,3},{... | collective-permute-start | bytes 307208 | tf_op jit(solution)/shard_map/ppermute | solution.py:36
  15.4 17.8 %all-to-all-start = ((s32[4,256,1]{1,2,0:T(1,128)}), s32[4,256,1]{1,2,0:T(1,128)S(1)}, u32[]{:S(2)}, u32[]{:S(2)}) async-start(s32[4,256,1]{1,2,0:T(1,128)} %compare_select_fusion.1), calls=%async_computation | async-start | bytes 8192 | tf_op jit(solution)/shard_map/all_to_all | solution.py:132
  23.8 1.2 %copy-start.1 = (s32[24]{0:T(128)S(1)}, s32[24]{0:T(128)}, u32[]{:S(2)}) copy-start(s32[24]{0:T(128)} %param.19) | copy-start | bytes 292
  32.2 1.8 %copy-start.28 = (f32[80]{0:T(128)S(1)}, f32[80]{0:T(128)}, u32[]{:S(2)}) copy-start(f32[80]{0:T(128)} %param.12) | copy-start | bytes 964
  33.3 0.6 copy-start.20
  33.3 0.6 copy-start.22
  36.7 3.2 %copy-start.2 = (f32[80,2048]{1,0:T(8,128)}, f32[80,2048]{1,0:T(8,128)S(1)}, u32[]{:S(2)}) copy-start(f32[80,2048]{1,0:T(8,128)S(1)} %convolution_bitcast_fusion.2) | copy-start | bytes 1966084
  40.1 4.1 %copy-start.21 = (bf16[80,640]{1,0:T(8,128)(2,1)S(1)}, bf16[80,640]{1,0:T(8,128)(2,1)}, u32[]{:S(2)}) copy-start(bf16[80,640]{1,0:T(8,128)(2,1)} %copy-done.20) | copy-start | bytes 307204
  40.1 4.8 %copy-start.23 = (bf16[80,640]{1,0:T(8,128)(2,1)S(1)}, bf16[80,640]{1,0:T(8,128)(2,1)}, u32[]{:S(2)}) copy-start(bf16[80,640]{1,0:T(8,128)(2,1)} %copy-done.22) | copy-start | bytes 307204
  40.3 5.4 %collective-permute-start.4 = (f32[80,256]{1,0:T(8,128)S(1)}, f32[80,256]{1,0:T(8,128)S(1)}, u32[]{:S(2)}, u32[]{:S(2)}) collective-permute-start(f32[80,256]{1,0:T(8,128)S(1)} %bitcast.157), channel_id=1, source_target_pairs={{0,4},{4,0},{8,12},{12,8},{1,5},{5,1},{9,13},{13,9},{2,6},{6,2},{1... | collective-permute-start | bytes 245768 | tf_op jit(solution)/shard_map/ppermute | solution.py:139
  41.9 5.3 %collective-permute-start.5 = (f32[80,256]{1,0:T(8,128)S(1)}, f32[80,256]{1,0:T(8,128)S(1)}, u32[]{:S(2)}, u32[]{:S(2)}) collective-permute-start(f32[80,256]{1,0:T(8,128)S(1)} %bitcast.158), channel_id=1, source_target_pairs={{0,8},{4,12},{8,0},{12,4},{1,9},{5,13},{9,1},{13,5},{2,10},{6,14},... | collective-permute-start | bytes 245768 | tf_op jit(solution)/shard_map/ppermute | solution.py:139
  44.1 5.2 %collective-permute-start.6 = (f32[80,256]{1,0:T(8,128)S(1)}, f32[80,256]{1,0:T(8,128)S(1)}, u32[]{:S(2)}, u32[]{:S(2)}) collective-permute-start(f32[80,256]{1,0:T(8,128)S(1)} %bitcast.159), channel_id=1, source_target_pairs={{0,12},{4,8},{8,4},{12,0},{1,13},{5,9},{9,5},{13,1},{2,14},{6,10},... | collective-permute-start | bytes 245768 | tf_op jit(solution)/shard_map/ppermute | solution.py:139
  44.9 5.1 %copy-start.4 = (pred[256,2304]{1,0:T(32,128)(4,1)S(1)}, pred[256,2304]{1,0:T(32,128)(4,1)}, u32[]{:S(2)}) copy-start(pred[256,2304]{1,0:T(32,128)(4,1)} %fusion.6) | copy-start | bytes 1769476
  49.3 1.5 %copy-start.8 = (f32[10,8,6,384]{3,1,2,0:T(8,128)S(1)}, f32[10,8,6,384]{3,1,2,0:T(8,128)}, u32[]{:S(2)}) copy-start(f32[10,8,6,384]{3,1,2,0:T(8,128)} %copy.135) | copy-start | bytes 2211844
  49.9 1.2 %copy-start.6 = (f32[80,2303]{1,0:T(8,128)S(1)}, f32[80,2303]{1,0:T(8,128)}, u32[]{:S(2)}) copy-start(f32[80,2303]{1,0:T(8,128)} %get-tuple-element.21) | copy-start | bytes 2210884
  49.9 1.4 %copy-start.7 = (f32[80,2303]{1,0:T(8,128)S(1)}, f32[80,2303]{1,0:T(8,128)}, u32[]{:S(2)}) copy-start(f32[80,2303]{1,0:T(8,128)} %get-tuple-element.22) | copy-start | bytes 2210884
  49.9 1.4 %copy-start.18 = (f32[80,384]{1,0:T(8,128)S(1)}, f32[80,384]{1,0:T(8,128)}, u32[]{:S(2)}) copy-start(f32[80,384]{1,0:T(8,128)} %slice_convert_fusion) | copy-start | bytes 368644
  50.0 1.4 %copy-start.19 = (f32[80,384]{1,0:T(8,128)S(1)}, f32[80,384]{1,0:T(8,128)}, u32[]{:S(2)}) copy-start(f32[80,384]{1,0:T(8,128)} %slice_convert_fusion.1) | copy-start | bytes 368644
  50.0 1.4 %copy-start.24 = (f32[80]{0:T(128)S(1)}, f32[80]{0:T(128)}, u32[]{:S(2)}) copy-start(f32[80]{0:T(128)} %param.14) | copy-start | bytes 964
  50.0 1.4 %copy-start.25 = (f32[80]{0:T(128)S(1)}, f32[80]{0:T(128)}, u32[]{:S(2)}) copy-start(f32[80]{0:T(128)} %param.13) | copy-start | bytes 964
  55.1 15.2 %collective-permute-start.9 = (bf16[80,6]{0,1:T(8,128)(2,1)S(1)}, bf16[80,6]{0,1:T(8,128)(2,1)S(1)}, u32[]{:S(2)}, u32[]{:S(2)}) collective-permute-start(bf16[80,6]{0,1:T(8,128)(2,1)S(1)} %bitcast.175), channel_id=1, source_target_pairs={{1,0},{2,1},{3,2},{5,4},{6,5},{7,6},{9,8},{10,9},{11,10},{13,12},{... | collective-permute-start | bytes 2888 | tf_op jit(solution)/shard_map/ppermute | solution.py:38
  59.9 11.6 %collective-permute-start.10 = (bf16[80,6]{0,1:T(8,128)(2,1)S(1)}, bf16[80,6]{0,1:T(8,128)(2,1)S(1)}, u32[]{:S(2)}, u32[]{:S(2)}) collective-permute-start(bf16[80,6]{0,1:T(8,128)(2,1)S(1)} %bitcast.173), channel_id=1, source_target_pairs={{0,1},{1,2},{2,3},{4,5},{5,6},{6,7},{8,9},{9,10},{10,11},{12,13},{... | collective-permute-start | bytes 2888 | tf_op jit(solution)/shard_map/ppermute | solution.py:37
  63.6 8.3 %collective-permute-start.7 = (bf16[80,384]{1,0:T(8,128)(2,1)S(1)}, bf16[80,384]{1,0:T(8,128)(2,1)S(1)}, u32[]{:S(2)}, u32[]{:S(2)}) collective-permute-start(bf16[80,384]{1,0:T(8,128)(2,1)S(1)} %bitcast.160), channel_id=1, source_target_pairs={{4,0},{8,4},{12,8},{5,1},{9,5},{13,9},{6,2},{10,6},{14,10},{7,3},{... | collective-permute-start | bytes 184328 | tf_op jit(solution)/shard_map/ppermute | solution.py:36
  64.9 7.0 %collective-permute-start.8 = (bf16[80,384]{1,0:T(8,128)(2,1)S(1)}, bf16[80,384]{1,0:T(8,128)(2,1)S(1)}, u32[]{:S(2)}, u32[]{:S(2)}) collective-permute-start(bf16[80,384]{1,0:T(8,128)(2,1)S(1)} %bitcast.162), channel_id=1, source_target_pairs={{0,4},{4,8},{8,12},{1,5},{5,9},{9,13},{2,6},{6,10},{10,14},{3,7},{... | collective-permute-start | bytes 184328 | tf_op jit(solution)/shard_map/ppermute | solution.py:35
  71.6 1.1 copy-start.15
  71.7 1.2 %copy-start.9 = (f32[80,2303]{1,0:T(8,128)S(1)}, f32[80,2303]{1,0:T(8,128)}, u32[]{:S(2)}) copy-start(f32[80,2303]{1,0:T(8,128)} %get-tuple-element.18) | copy-start | bytes 2210884
  71.8 1.4 %copy-start.11 = (f32[10,8,6,384]{3,1,2,0:T(8,128)S(1)}, f32[10,8,6,384]{3,1,2,0:T(8,128)}, u32[]{:S(2)}) copy-start(f32[10,8,6,384]{3,1,2,0:T(8,128)} %copy.137) | copy-start | bytes 2211844
  71.8 1.6 %copy-start.14 = (f32[80,1920]{1,0:T(8,128)S(1)}, f32[80,1920]{1,0:T(8,128)}, u32[]{:S(2)}) copy-start(f32[80,1920]{1,0:T(8,128)} %get-tuple-element.19) | copy-start | bytes 1843204
  75.6 12.4 %collective-permute-start.13 = (bf16[80,6]{0,1:T(8,128)(2,1)S(1)}, bf16[80,6]{0,1:T(8,128)(2,1)S(1)}, u32[]{:S(2)}, u32[]{:S(2)}) collective-permute-start(bf16[80,6]{0,1:T(8,128)(2,1)S(1)} %bitcast.176), channel_id=1, source_target_pairs={{1,0},{2,1},{3,2},{5,4},{6,5},{7,6},{9,8},{10,9},{11,10},{13,12},{... | collective-permute-start | bytes 2888 | tf_op jit(solution)/shard_map/ppermute | solution.py:38
  78.0 11.3 %collective-permute-start.14 = (bf16[80,6]{0,1:T(8,128)(2,1)S(1)}, bf16[80,6]{0,1:T(8,128)(2,1)S(1)}, u32[]{:S(2)}, u32[]{:S(2)}) collective-permute-start(bf16[80,6]{0,1:T(8,128)(2,1)S(1)} %bitcast.174), channel_id=1, source_target_pairs={{0,1},{1,2},{2,3},{4,5},{5,6},{6,7},{8,9},{9,10},{10,11},{12,13},{... | collective-permute-start | bytes 2888 | tf_op jit(solution)/shard_map/ppermute | solution.py:37
  81.6 8.2 %collective-permute-start.11 = (bf16[80,384]{1,0:T(8,128)(2,1)S(1)}, bf16[80,384]{1,0:T(8,128)(2,1)S(1)}, u32[]{:S(2)}, u32[]{:S(2)}) collective-permute-start(bf16[80,384]{1,0:T(8,128)(2,1)S(1)} %bitcast.161), channel_id=1, source_target_pairs={{4,0},{8,4},{12,8},{5,1},{9,5},{13,9},{6,2},{10,6},{14,10},{7,3},{... | collective-permute-start | bytes 184328 | tf_op jit(solution)/shard_map/ppermute | solution.py:36
  82.9 6.9 %collective-permute-start.12 = (bf16[80,384]{1,0:T(8,128)(2,1)S(1)}, bf16[80,384]{1,0:T(8,128)(2,1)S(1)}, u32[]{:S(2)}, u32[]{:S(2)}) collective-permute-start(bf16[80,384]{1,0:T(8,128)(2,1)S(1)} %bitcast.163), channel_id=1, source_target_pairs={{0,4},{4,8},{8,12},{1,5},{5,9},{9,13},{2,6},{6,10},{10,14},{3,7},{... | collective-permute-start | bytes 184328 | tf_op jit(solution)/shard_map/ppermute | solution.py:35
  89.6 1.1 copy-start.10
  89.6 1.3 %copy-start.12 = (f32[80,1920]{1,0:T(8,128)S(1)}, f32[80,1920]{1,0:T(8,128)}, u32[]{:S(2)}) copy-start(f32[80,1920]{1,0:T(8,128)} %get-tuple-element.15) | copy-start | bytes 1843204
  89.6 1.5 %copy-start.13 = (f32[80,1920]{1,0:T(8,128)S(1)}, f32[80,1920]{1,0:T(8,128)}, u32[]{:S(2)}) copy-start(f32[80,1920]{1,0:T(8,128)} %get-tuple-element.16) | copy-start | bytes 1843204
  91.0 1.3 %copy-start.5 = (pred[256,2304]{1,0:T(32,128)(4,1)S(1)}, pred[256,2304]{1,0:T(32,128)(4,1)}, u32[]{:S(2)}) copy-start(pred[256,2304]{1,0:T(32,128)(4,1)} %fusion.6) | copy-start | bytes 1769476
  94.4 13.8 %all-to-all-start.1 = ((f32[80,4,256]{2,0,1:T(8,128)}), f32[80,4,256]{2,0,1:T(8,128)S(1)}, u32[]{:S(2)}, u32[]{:S(2)}) async-start(f32[80,4,256]{2,0,1:T(8,128)} %broadcast_select_fusion.1), calls=%async_computation.1 | async-start | bytes 655360 | tf_op jit(solution)/shard_map/all_to_all | solution.py:181
  114.8 1.1 copy-start.3
  114.8 1.1 copy-start.29
